TPU v7x, 32 devices: a whole 2x2x4 slice. The times are simulated.
32 devices in a mesh: grp: 2 (over x), tile: 16 (over z, y, core).
Axes of the slice: x: 2, y: 2, z: 4, core: 2. Of those that a mesh axis runs over, the one named last changes fastest.
Arguments:
- latent: float32 [32, 1024, 128], P(None, ('grp', 'tile')), parts along dimension 1, may hold values from -6 to 6
- observed: float32 [32, 1024, 128], P(None, ('grp', 'tile')), parts along dimension 1, may hold values from -6 to 6
- noise: float32 [32, 1024, 128], P(None, ('grp', 'tile')), parts along dimension 1, may hold values from -6 to 6
- cloudy: int32 [128], P(('grp', 'tile')), parts along dimension 0, may hold values from 0 to 1, as said below
- timestep: int32 [2], P('grp'), parts along dimension 0, may hold values from 200 to 800
- pos_embed: bfloat16 [256, 2048], replicated, may hold values from -3 to 3
- embed_w: bfloat16 [128, 2048], replicated, may hold values from -0.5 to 0.5
- mod_w: bfloat16 [256, 6144], P(None, 'tile'), may hold values from -0.375 to 0.375
- wq: bfloat16 [2048, 1024], P('tile')
- wk: bfloat16 [2048, 1024], P('tile')
- wv: bfloat16 [2048, 1024], P('tile'), may hold values from -0.125 to 0.125
- wo: bfloat16 [1024, 2048], P(None, 'tile'), may hold values from -0.1875 to 0.1875
- q_gain: float32 [128], replicated, may hold values from 0.6 to 4.2
- k_gain: float32 [128], replicated, may hold values from 0.6 to 4.2
- out_w: bfloat16 [2048, 128], replicated, may hold values from -0.125 to 0.125
- conv_w: float32 [9, 32, 32], replicated, may hold values from -0.375 to 0.375
Outputs:
- estimate: float32 [32, 1024, 128], P(None, ('grp', 'tile')), parts along dimension 1
- next_latent: float32 [32, 1024, 128], P(None, ('grp', 'tile')), parts along dimension 1
There are 2 independent parts, one for each index of `grp`. A program takes and returns all parts, laid end to end along the dimension named above; an argument that names none is the same for every part. Nothing has to cross between parts.
Inputs may be any that keep to these rules, and one draw needn't show every extreme that they name: Exactly 16 tiles of a part are cloudy; each band of 4 tiles holds at most 3 of them, and some band holds exactly 3.
All inputs are finite; a program needn't handle non-finite values.
Results may differ from a plain program's by a relative error of at most 0.0033.
Values may be sent and summed in bfloat16 or wider, within the bound.
No kernel may reach another device: no remote copies, remote signals or barrier semaphores. Data moves between devices by JAX's collectives and lax.ppermute only.
A program may use at most 128 MiB of HBM per device.

v0:
```python
import math
import jax
import jax.numpy as jnp
from jax import lax
from jax.sharding import PartitionSpec as P

HD = 128
PATCH = 2
MAXOWN = 3
TSTEPS = 1000
STRIDE = 20


def padded_2(block, sides, width):
    for axis, dim in sides:
        count = lax.axis_size(axis)
        forward = [(i, i + 1) for i in range(count - 1)]
        backward = [(target, source) for source, target in forward]
        low = lax.ppermute(
            lax.slice_in_dim(block, block.shape[dim] - width, None, axis=dim), axis, forward
        )
        high = lax.ppermute(lax.slice_in_dim(block, 0, width, axis=dim), axis, backward)
        block = jnp.concatenate([low, block, high], axis=dim)
    return block


def plan(step):
    theta = (step / TSTEPS + 0.008) / 1.008 * (math.pi / 2)
    return (jnp.cos(theta), jnp.sin(theta))


def time_features(step, width):
    half = width // 2
    freqs = jnp.exp(-math.log(10000.0) * jnp.arange(half, dtype=jnp.float32) / half)
    angles = step * freqs
    code = jnp.concatenate([jnp.cos(angles), jnp.sin(angles)])[None, :]
    return jax.nn.silu(code).astype(jnp.bfloat16)


def layer_norm(values):
    center = values - jnp.mean(values, axis=-1, keepdims=True)
    spread = jnp.mean(center * center, axis=-1, keepdims=True)
    return center * lax.rsqrt(spread + 1e-06)


def head_norm(proj, gain, count, tokens_tile):
    shaped = proj.reshape(count, tokens_tile, -1, HD)
    scaled = shaped * lax.rsqrt(jnp.mean(shaped * shaped, axis=-1, keepdims=True) + 1e-06)
    return (scaled * gain).astype(jnp.bfloat16)


def band_tiles(band, tile_side):
    channels, band_rows, band_cols = band.shape
    tiles_here = band_cols // (tile_side * PATCH)
    shaped = band.reshape(channels, tile_side, PATCH, tiles_here, tile_side, PATCH)
    return jnp.transpose(shaped, (3, 1, 4, 2, 5, 0)).reshape(
        tiles_here, tile_side * tile_side, PATCH * PATCH * channels
    )


def band_pixels(tiled, tile_side, channels):
    tiles_here = tiled.shape[0]
    shaped = tiled.reshape(tiles_here, tile_side, tile_side, PATCH, PATCH, channels)
    return jnp.transpose(shaped, (5, 1, 3, 0, 2, 4)).reshape(
        channels, tile_side * PATCH, tiles_here * tile_side * PATCH
    )


def add_rows(left, shard_rows):
    return jnp.dot(left, shard_rows, preferred_element_type=jnp.float32)


def denoise(
    chosen,
    embed_w,
    pos_embed,
    shift_vec,
    scale_vec,
    gate_vec,
    wq,
    wk,
    wv,
    wo,
    q_gain,
    k_gain,
    out_w,
):
    count, tokens_tile, token_values = chosen.shape
    row_count = count * tokens_tile
    flat = chosen.reshape(row_count, token_values)
    hidden0 = jnp.dot(flat, embed_w, preferred_element_type=jnp.float32).reshape(
        count, tokens_tile, -1
    )
    hidden0 = (hidden0 + pos_embed.astype(jnp.float32)[None]).reshape(row_count, -1)
    modulated = (layer_norm(hidden0) * (1.0 + scale_vec) + shift_vec).astype(jnp.bfloat16)

    def add_one(shard_rows):
        return add_rows(modulated, shard_rows)

    query_all = add_one(lax.all_gather(wq, "tile", axis=0, tiled=True))
    key_all = add_one(lax.all_gather(wk, "tile", axis=0, tiled=True))
    value_all = add_one(lax.all_gather(wv, "tile", axis=0, tiled=True))
    query_norm = head_norm(query_all, q_gain, count, tokens_tile)
    key_norm = head_norm(key_all, k_gain, count, tokens_tile)
    value_half = value_all.reshape(count, tokens_tile, -1, HD).astype(jnp.bfloat16)
    scores = jnp.einsum(
        "nqhd,nkhd->nhqk", query_norm, key_norm, preferred_element_type=jnp.float32
    ) * HD ** (-0.5)
    peak = jnp.max(scores, axis=-1, keepdims=True)
    expo = jnp.exp(scores - peak)
    probs = (expo / jnp.sum(expo, axis=-1, keepdims=True)).astype(jnp.bfloat16)
    mixed = jnp.einsum("nhqk,nkhd->nqhd", probs, value_half, preferred_element_type=jnp.float32)
    mixed = mixed.astype(jnp.bfloat16).reshape(row_count, -1)
    attn_out = jnp.dot(
        mixed, lax.all_gather(wo, "tile", axis=1, tiled=True), preferred_element_type=jnp.float32
    )
    hidden1 = hidden0 + gate_vec * attn_out
    final = layer_norm(hidden1).astype(jnp.bfloat16)
    eps_pred = jnp.dot(final, out_w, preferred_element_type=jnp.float32).astype(jnp.bfloat16)
    return eps_pred.reshape(count, tokens_tile, token_values)


def on_device(
    latent,
    observed,
    noise,
    cloudy,
    timestep,
    pos_embed,
    embed_w,
    mod_w,
    wq,
    wk,
    wv,
    wo,
    q_gain,
    k_gain,
    out_w,
    conv_w,
):
    channels, band_rows, band_cols = latent.shape
    tile_side = band_rows // PATCH
    tiles_here = band_cols // band_rows
    width = embed_w.shape[1]
    step_now = timestep[0].astype(jnp.float32)
    cos_now, sin_now = plan(step_now)
    cos_prev, sin_prev = plan(step_now - STRIDE)
    time_code = time_features(step_now, mod_w.shape[0])
    local_mod = jnp.dot(time_code, mod_w, preferred_element_type=jnp.float32)
    modulation = lax.all_gather(local_mod, "tile", axis=1, tiled=True)
    shift_vec = modulation[:, :width]
    scale_vec = modulation[:, width : 2 * width]
    gate_vec = modulation[:, 2 * width :]
    tile_tokens = band_tiles(latent.astype(jnp.bfloat16), tile_side)
    order_in = jnp.cumsum(cloudy) - cloudy
    weights_all = (
        embed_w,
        pos_embed,
        shift_vec,
        scale_vec,
        gate_vec,
        wq,
        wk,
        wv,
        wo,
        q_gain,
        k_gain,
        out_w,
    )
    slot_ids = jnp.arange(MAXOWN, dtype=jnp.int32)
    slot_hit = (cloudy[None, :] == 1) & (order_in[None, :] == slot_ids[:, None])
    picked = jnp.sum(
        jnp.where(slot_hit, jnp.arange(tiles_here, dtype=jnp.int32)[None, :], 0), axis=1
    )
    chosen = jnp.take(tile_tokens, picked, axis=0)
    eps_chosen = denoise(chosen, *weights_all)
    eps_back = jnp.take(eps_chosen, jnp.minimum(order_in, MAXOWN - 1), axis=0)
    eps_tiles = jnp.where(cloudy[:, None, None] == 1, eps_back, jnp.zeros_like(eps_back))
    eps_latent = band_pixels(eps_tiles.astype(jnp.float32), tile_side, channels)
    cloud_cols = jnp.repeat(cloudy, band_rows) == 1
    raw_estimate = jnp.where(
        cloud_cols[None, None, :], (latent - sin_now * eps_latent) / cos_now, observed
    )
    padded = padded_2(raw_estimate, (("tile", 1),), 1)
    padded = jnp.pad(padded, ((0, 0), (0, 0), (1, 1)))
    blended = jnp.zeros_like(raw_estimate)
    for row_shift in range(3):
        for col_shift in range(3):
            window = padded[:, row_shift : row_shift + band_rows, col_shift : col_shift + band_cols]
            blended = blended + jnp.einsum(
                "oc,chw->ohw",
                conv_w[3 * row_shift + col_shift],
                window,
                precision=lax.Precision.HIGHEST,
            )
    row_pos = jnp.arange(band_rows) % band_rows
    col_pos = jnp.arange(band_cols) % band_rows
    seam_mask = ((row_pos == 0) | (row_pos == band_rows - 1))[:, None] | (
        (col_pos == 0) | (col_pos == band_rows - 1)
    )[None, :]
    estimate = jnp.where(seam_mask[None], blended, raw_estimate)
    next_latent = cos_prev * estimate + sin_prev * noise
    return (estimate, next_latent)


def solution(mesh):
    placed = (
        P(None, ("grp", "tile"), None),
        P(None, ("grp", "tile"), None),
        P(None, ("grp", "tile"), None),
        P(("grp", "tile")),
        P("grp"),
        P(),
        P(),
        P(None, "tile"),
        P("tile", None),
        P("tile", None),
        P("tile", None),
        P(None, "tile"),
        P(),
        P(),
        P(),
        P(),
    )
    return jax.shard_map(
        on_device,
        mesh=mesh,
        in_specs=placed,
        out_specs=(P(None, ("grp", "tile"), None), P(None, ("grp", "tile"), None)),
        check_vma=False,
    )
```

profile of v0, /device:TPU:1, one launch (start us, length us, event | category | flops | bytes accessed | tf_op | source)
XLA Modules:
  0.0 257.6 jit_solution(8507005595487570797)
XLA Ops:
  7.2 0.7 all-gather.11.cloned.1.call-update
  8.0 0.7 all-gather.9.cloned.1.call-update
  8.7 0.7 all-gather.7.cloned.1.call-update
  10.0 0.8 reduce-window.9
  10.8 0.7 compare_and_fusion.1
  12.3 1.1 convolution_bitcast_fusion
  13.6 1.5 copy.77
  15.1 1.1 copy.78
  16.8 1.5 convert_element_type.57
  18.4 0.6 gather_fusion
  19.0 23.0 %all-gather.1 = f32[16,1,384]{2,1,0:T(1,128)S(1)} all-gather(f32[1,1,384]{2,1,0:T(1,128)S(1)} %convolution_bitcast_fusion), channel_id=2, replica_groups=mesh['grp'=2,'tile'=16] {'tile'}, dimensions={0}, use_global_device_ids=true | all-gather | bytes 26112 | tf_op jit(solution)/shard_map/all_gather | solution.py:150
  42.1 1.1 fusion.72
  43.2 0.8 multiply_reduce_fusion.1
  44.0 1.8 copy-done.2
  45.8 2.8 %fusion.4 = bf16[3,256,2048,1]{2,1,3,0:T(8,128)(2,1)} fusion(f32[3,256,2048]{2,1,0:T(8,128)S(1)} %get-tuple-element.22, f32[2048]{0:T(1024)S(1)} %bitcast.119, f32[2048]{0:T(1024)S(1)} %bitcast.118, f32[3,256]{1,0:T(4,128)S(1)} %add_rsqrt_fusion.3, f32[3,256]{1,0:T(4,128)S(1)} %broadcast_multiply_fusion.1), kind=kLoop, calls=%fused_computation.13 | loop fusion | flops 7864320 | bytes 9459712 | tf_op jit(solution)/shard_map/convert_element_type | solution.py:95
  48.7 14.8 %all-gather.11.cloned.1.call-done = bf16[2048,1024]{1,0:T(8,128)(2,1)} async-done(((bf16[128,1024]{1,0:T(8,128)(2,1)}), bf16[2048,1024]{1,0:T(8,128)(2,1)}) %all-gather.11.cloned.1.call-update) | async-done | bytes 4194320 | tf_op jit(solution)/shard_map/all_gather | solution.py:101
  63.5 6.5 %copy.81 = bf16[1024,2048]{1,0:T(8,128)(2,1)} copy(bf16[1024,2048]{0,1:T(8,128)(2,1)} %bitcast.108) | data formatting | bytes 8388608 | tf_op jit(solution)/shard_map/dot_general | solution.py:70
  70.0 44.7 %all-gather.9.cloned.1.call-done = bf16[2048,1024]{1,0:T(8,128)(2,1)} async-done(((bf16[128,1024]{1,0:T(8,128)(2,1)}), bf16[2048,1024]{1,0:T(8,128)(2,1)}) %all-gather.9.cloned.1.call-update) | async-done | bytes 4194320 | tf_op jit(solution)/shard_map/all_gather | solution.py:100
  114.7 6.5 %copy.80 = bf16[1024,2048]{1,0:T(8,128)(2,1)} copy(bf16[1024,2048]{0,1:T(8,128)(2,1)} %bitcast.109) | data formatting | bytes 8388608 | tf_op jit(solution)/shard_map/dot_general | solution.py:70
  121.2 44.7 %all-gather.7.cloned.1.call-done = bf16[2048,1024]{1,0:T(8,128)(2,1)} async-done(((bf16[128,1024]{1,0:T(8,128)(2,1)}), bf16[2048,1024]{1,0:T(8,128)(2,1)}) %all-gather.7.cloned.1.call-update) | async-done | bytes 4194320 | tf_op jit(solution)/shard_map/all_gather | solution.py:102
  166.0 6.5 %copy.79 = bf16[1024,2048]{1,0:T(8,128)(2,1)} copy(bf16[1024,2048]{0,1:T(8,128)(2,1)} %bitcast.110) | data formatting | bytes 8388608 | tf_op jit(solution)/shard_map/dot_general | solution.py:70
  172.4 6.6 %multiply_reduce_fusion.3 = (f32[3,256,8]{1,2,0:T(8,128)S(1)}, f32[3,256,8,128]{1,3,2,0:T(8,128)S(1)}) fusion(bf16[3,256,2048,1]{2,1,3,0:T(8,128)(2,1)} %fusion.4, bf16[8,128,2048,1]{2,1,0,3:T(8,128)(2,1)} %bitcast.113), kind=kOutput, calls=%fused_computation.19 | convolution fusion | flops 3222792192 | bytes 10510336 | tf_op jit(solution)/shard_map/dot_general | solution.py:70
  179.1 3.5 %multiply_reduce_fusion.4 = (f32[3,256,8]{1,2,0:T(8,128)S(1)}, f32[3,256,8,128]{1,3,2,0:T(8,128)S(1)}) fusion(bf16[3,256,2048,1]{2,1,3,0:T(8,128)(2,1)S(1)} %copy-done.4, bf16[8,128,2048,1]{2,1,0,3:T(8,128)(2,1)S(1)} %bitcast.112), kind=kOutput, calls=%fused_computation.21 | convolution fusion | flops 3222792192 | bytes 10510336 | tf_op jit(solution)/shard_map/dot_general | solution.py:70
  182.6 1.3 fusion.11
  183.9 4.3 %fusion.73 = (f32[3,8,256]{2,1,0:T(8,128)S(1)}, f32[3,8,256,256]{2,3,1,0:T(8,128)}) fusion(f32[3,8,256,256]{2,3,1,0:T(8,128)S(1)} %fusion.11), kind=kOutput, calls=%fused_computation.131 | output fusion | flops 6291711 | bytes 12607488 | tf_op jit(solution)/shard_map/sub | solution.py:110
  188.2 10.3 %fusion.18 = bf16[3,256,8,128]{1,3,2,0:T(8,128)(2,1)} fusion(f32[3,8,256,256]{2,3,1,0:T(8,128)} %get-tuple-element.28, f32[3,8,256]{2,1,0:T(8,128)S(1)} %get-tuple-element.27, bf16[3,256,2048,1]{2,1,3,0:T(8,128)(2,1)} %fusion.4, bf16[8,128,2048,1]{2,1,0,3:T(8,128)(2,1)} %bitcast.111), kind=kOutput, calls=%fused_computation.37 | convolution fusion | flops 3628597248 | bytes 15228928 | tf_op jit(solution)/shard_map/nhqk,nkhd->nqhd/dot_general | solution.py:112
  198.5 2.0 copy.86
  200.5 19.2 %all-gather.13.cloned.1.call-done = bf16[1024,2048]{1,0:T(8,128)(2,1)} async-done(((bf16[1024,128]{1,0:T(8,128)(2,1)}), bf16[1024,2048]{1,0:T(8,128)(2,1)}) %all-gather.13.cloned.1.call-update) | async-done | bytes 4194320 | tf_op jit(solution)/shard_map/all_gather | solution.py:115
  219.7 7.0 %fusion.74 = (f32[768]{0:T(1024)S(1)}, f32[768,2048]{1,0:T(8,128)S(1)}) fusion(bf16[1024,2048]{1,0:T(8,128)(2,1)} %all-gather.13.cloned.1.call-done, bf16[96,8,8,128]{3,2,1,0:T(8,128)(2,1)S(1)} %bitcast.115, f32[2048]{0:T(1024)S(1)} %bitcast.120, f32[3,256,2048]{2,1,0:T(8,128)} %copy-done.2), kind=kOutput, calls=%fused_computation.132 | convolution fusion | flops 3225943296 | bytes 18361344 | tf_op jit(solution)/shard_map/dot_general | solution.py:114
  226.7 0.8 multiply_reduce_fusion
  227.8 1.1 fusion.22
  228.9 0.6 gather_fusion.1
  229.9 1.1 multiply_bitcast_fusion
  231.0 1.1 copy.87
  232.1 0.6 copy.89
  232.7 1.6 copy_select_fusion
  234.4 3.2 %collective-permute-start = (f32[32,1,128]{2,0,1:T(8,128)S(1)}, f32[32,1,128]{2,0,1:T(8,128)S(1)}, u32[]{:S(2)}, u32[]{:S(2)}) collective-permute-start(f32[32,1,128]{2,0,1:T(8,128)S(1)} %get-tuple-element.15), channel_id=1, source_target_pairs={{0,1},{1,2},{2,3},{3,4},{4,5},{5,6},{6,7},{7,8},{8,9},{9,10},{10,1... | collective-permute-start | bytes 49160 | tf_op jit(solution)/shard_map/ppermute | solution.py:19
  237.5 2.2 collective-permute-start.1
  240.0 2.6 %collective-permute-done.1 = f32[32,1,128]{2,0,1:T(8,128)S(1)} collective-permute-done((f32[32,1,128]{2,0,1:T(8,128)S(1)}, f32[32,1,128]{2,0,1:T(8,128)S(1)}, u32[]{:S(2)}, u32[]{:S(2)}) %collective-permute-start.1) | collective-permute-done | bytes 16416 | tf_op jit(solution)/shard_map/ppermute | solution.py:22
  243.0 0.7 fusion.31
  244.8 0.7 convolution_add_fusion.6
  245.5 0.6 convolution_add_fusion.5
  246.1 0.6 convolution_add_fusion.4
  246.7 0.7 convolution_add_fusion.3
  247.4 0.6 convolution_add_fusion.2
  248.0 0.9 fusion.39
  248.9 1.1 copy.92
  250.0 1.1 copy.93
  (53 shorter events, 3.9 us)
Async XLA Ops:
  7.2 34.9 %copy-start = (bf16[128,2048]{1,0:T(8,128)(2,1)S(1)}, bf16[128,2048]{1,0:T(8,128)(2,1)}, u32[]{:S(2)}) copy-start(bf16[128,2048]{1,0:T(8,128)(2,1)} %param.22) | copy-start | bytes 1572868
  7.2 56.3 %all-gather.11.cloned.1.call-start = ((), (), s32[]{:S(2)}) async-start(), calls=%async_computation.2 | async-start | bytes 4456448 | tf_op jit(solution)/shard_map/all_gather | solution.py:101
  7.9 106.8 %all-gather.9.cloned.1.call-start = ((), (), s32[]{:S(2)}) async-start(), calls=%async_computation.1 | async-start | bytes 4456448 | tf_op jit(solution)/shard_map/all_gather | solution.py:100
  8.7 157.3 %all-gather.7.cloned.1.call-start = ((), (), s32[]{:S(2)}) async-start(), calls=%async_computation | async-start | bytes 4456448 | tf_op jit(solution)/shard_map/all_gather | solution.py:102
  9.4 210.3 %all-gather.13.cloned.1.call-start = ((), (), s32[]{:S(2)}) async-start(), calls=%async_computation.3 | async-start | bytes 4456448 | tf_op jit(solution)/shard_map/all_gather | solution.py:115
  43.2 2.7 %copy-start.2 = (f32[3,256,2048]{2,1,0:T(8,128)}, f32[3,256,2048]{2,1,0:T(8,128)S(1)}, u32[]{:S(2)}) copy-start(f32[3,256,2048]{2,1,0:T(8,128)S(1)} %get-tuple-element.22) | copy-start | bytes 18874372
  172.4 6.7 %copy-start.3 = (bf16[1024,2048]{1,0:T(8,128)(2,1)S(1)}, bf16[1024,2048]{1,0:T(8,128)(2,1)}, u32[]{:S(2)}) copy-start(bf16[1024,2048]{1,0:T(8,128)(2,1)} %copy.80) | copy-start | bytes 12582916
  172.4 6.7 %copy-start.4 = (bf16[3,256,2048,1]{2,1,3,0:T(8,128)(2,1)S(1)}, bf16[3,256,2048,1]{2,1,3,0:T(8,128)(2,1)}, u32[]{:S(2)}) copy-start(bf16[3,256,2048,1]{2,1,3,0:T(8,128)(2,1)} %fusion.4) | copy-start | bytes 9437188
  179.1 3.5 %copy-start.9 = (f32[128]{0:T(128)S(1)}, f32[128]{0:T(128)}, u32[]{:S(2)}) copy-start(f32[128]{0:T(128)} %param.29) | copy-start | bytes 1540
  179.1 3.5 %copy-start.10 = (f32[128]{0:T(128)S(1)}, f32[128]{0:T(128)}, u32[]{:S(2)}) copy-start(f32[128]{0:T(128)} %param.28) | copy-start | bytes 1540
  226.7 1.0 copy-start.7
  230.9 1.8 copy-start.5
  232.1 10.8 %copy-start.8 = (f32[9,32,32]{2,1,0:T(8,128)S(1)}, f32[9,32,32]{2,1,0:T(8,128)}, u32[]{:S(2)}) copy-start(f32[9,32,32]{2,1,0:T(8,128)} %param.31) | copy-start | bytes 110596
  234.4 5.6 %collective-permute-start = (f32[32,1,128]{2,0,1:T(8,128)S(1)}, f32[32,1,128]{2,0,1:T(8,128)S(1)}, u32[]{:S(2)}, u32[]{:S(2)}) collective-permute-start(f32[32,1,128]{2,0,1:T(8,128)S(1)} %get-tuple-element.15), channel_id=1, source_target_pairs={{0,1},{1,2},{2,3},{3,4},{4,5},{5,6},{6,7},{7,8},{8,9},{9,10},{10,1... | collective-permute-start | bytes 49160 | tf_op jit(solution)/shard_map/ppermute | solution.py:19
  237.5 5.1 %collective-permute-start.1 = (f32[32,1,128]{2,0,1:T(8,128)S(1)}, f32[32,1,128]{2,0,1:T(8,128)S(1)}, u32[]{:S(2)}, u32[]{:S(2)}) collective-permute-start(f32[32,1,128]{2,0,1:T(8,128)S(1)} %get-tuple-element.16), channel_id=1, source_target_pairs={{1,0},{2,1},{3,2},{4,3},{5,4},{6,5},{7,6},{8,7},{9,8},{10,9},{11,1... | collective-permute-start | bytes 49160 | tf_op jit(solution)/shard_map/ppermute | solution.py:22
  245.5 2.5 copy-start.6
  247.4 3.7 %copy-start.1 = (bf16[128,2048]{1,0:T(8,128)(2,1)S(1)}, bf16[128,2048]{1,0:T(8,128)(2,1)}, u32[]{:S(2)}) copy-start(bf16[128,2048]{1,0:T(8,128)(2,1)} %param.22) | copy-start | bytes 1572868
Sparse Core Ops, SparseCore 0:
  10.2 53.2 all-gather.10
  65.6 49.0 all-gather.8
  116.9 49.0 all-gather.6
  168.0 51.7 all-gather.12
where the time goes:
time: 258 us
  waiting for transfers between devices  129 us (50%)
  matrix products  37.7 us (15%)
  local copies, waits for them, and re-layouts  32.5 us (13%)
  blocking collectives  23 us (9%)
  between operations  15.2 us (6%)
  other arithmetic  15 us (6%)
  starting transfers between devices  5.5 us (2%)
    all_gather x1, waiting for transfers between devices, denoise(): value_all = add_one(lax.all_gather(wv, 'tile', axis=0, tiled=True))  44.7 us
    all_gather x1, waiting for transfers between devices, denoise(): query_all = add_one(lax.all_gather(wq, 'tile', axis=0, tiled=True))  44.7 us
    all_gather x1, blocking collectives, on_device(): modulation = lax.all_gather(local_mod, 'tile', axis=1, tiled=True)  23 us
    dot_general x3, local copies, waits for them, and re-layouts, add_rows(): return jnp.dot(left, shard_rows, preferred_element_type=jnp.float32)  19.5 us
    all_gather x1, waiting for transfers between devices, denoise(): lax.all_gather(wo, 'tile', axis=1, tiled=True)  19.2 us
    all_gather x1, waiting for transfers between devices, denoise(): key_all = add_one(lax.all_gather(wk, 'tile', axis=0, tiled=True))  14.8 us
    dot_general x1, matrix products, denoise(): jnp.einsum('nhqk,nkhd->nqhd', probs, value_half, preferred_element_type=j...  10.3 us
    dot_general x2, matrix products, add_rows(): return jnp.dot(left, shard_rows, preferred_element_type=jnp.float32)  10.1 us
  transfers between devices with their start and end apart: 6, of which 5 were waited for; matrix products, arithmetic and copies ran while one was open for 23% of the time, Pallas kernels for 0%

commit v1 on v0

--- a/solution.py
+++ b/solution.py
@@ -9,6 +9,23 @@
 MAXOWN = 3
 TSTEPS = 1000
 STRIDE = 20
+
+
+def watch_area_for(my_tile):
+    n = lax.axis_size("tile")
+    carry_in = range(1, n)
+    b_next = map(lambda dev_i: (dev_i - 1, dev_i), carry_in)
+    reply = list(b_next)
+    z1 = reply + [(n - 1, 0)]
+    piece_out = my_tile
+    pieces_in = [piece_out]
+    for _ in [*range(n - 1)]:
+        piece_out = lax.ppermute(piece_out, "tile", z1)
+        pieces_in += [piece_out]
+    answer = jnp.concatenate([*reversed(pieces_in)], axis=1)
+    w2 = lax.axis_index("tile")
+    block_next = jnp.roll(answer, (w2 + 1) * piece_out.shape[1], axis=1)
+    return block_next
 
 
 def padded_2(block, sides, width):
@@ -147,7 +164,7 @@
     cos_prev, sin_prev = plan(step_now - STRIDE)
     time_code = time_features(step_now, mod_w.shape[0])
     local_mod = jnp.dot(time_code, mod_w, preferred_element_type=jnp.float32)
-    modulation = lax.all_gather(local_mod, "tile", axis=1, tiled=True)
+    modulation = watch_area_for(local_mod)
     shift_vec = modulation[:, :width]
     scale_vec = modulation[:, width : 2 * width]
     gate_vec = modulation[:, 2 * width :]

time: 258 us -> 258 us (level)
  blocking collectives: 23 us -> 0 us
  waiting for transfers between devices: 129 us -> 144 us
  starting transfers between devices: 5.5 us -> 11.7 us
  other arithmetic: 15 us -> 18 us
    ppermute x0 -> x15, waiting for transfers between devices: none -> 66.6 us  [watch_area_for(): piece_out = lax.ppermute(piece_out, 'tile', z1)]
    all_gather x1, waiting for transfers between devices: 44.7 us -> 8.64 us  [denoise(): query_all = add_one(lax.all_gather(wq, 'tile', axis=0, tiled=True))]
    all_gather x1 -> x0, blocking collectives: 23 us -> none  [on_device(): modulation = lax.all_gather(local_mod, 'tile', axis=1, tiled=True)]
    all_gather x1, waiting for transfers between devices: 14.8 us -> 0.01 us  [denoise(): key_all = add_one(lax.all_gather(wk, 'tile', axis=0, tiled=True))]
    ppermute x0 -> x15, starting transfers between devices: none -> 6.17 us  [watch_area_for(): piece_out = lax.ppermute(piece_out, 'tile', z1)]
    convert_element_type x1, other arithmetic: 2.83 us -> 5.69 us  [denoise(): (layer_norm(hidden0) * (1.0 + scale_vec) + shift_vec).astype(jnp.bfloat16)]
    unnamed x25 -> x56, local copies, waits for them, and re-layouts: 5.88 us -> 4.31 us
  transfers between devices with their start and end apart: 6 -> 21, of which waited for: 5 -> 19; matrix products, arithmetic and copies ran while one was open for 23% -> 25% of each run, Pallas kernels for 0% -> 0%
where the time goes in v1:
time: 258 us; the launch traced here: 257 us
  waiting for transfers between devices  144 us (56%)
  matrix products  37.7 us (15%)
  local copies, waits for them, and re-layouts  31 us (12%)
  other arithmetic  18 us (7%)
  between operations  15.3 us (6%)
  starting transfers between devices  11.7 us (5%)
    ppermute x15, waiting for transfers between devices, watch_area_for(): piece_out = lax.ppermute(piece_out, 'tile', z1)  66.6 us
    all_gather x1, waiting for transfers between devices, denoise(): value_all = add_one(lax.all_gather(wv, 'tile', axis=0, tiled=True))  44.7 us
    dot_general x3, local copies, waits for them, and re-layouts, add_rows(): return jnp.dot(left, shard_rows, preferred_element_type=jnp.float32)  19.5 us
    all_gather x1, waiting for transfers between devices, denoise(): lax.all_gather(wo, 'tile', axis=1, tiled=True)  19.3 us
    dot_general x1, matrix products, denoise(): jnp.einsum('nhqk,nkhd->nqhd', probs, value_half, preferred_element_type=j...  10.3 us
    dot_general x2, matrix products, add_rows(): return jnp.dot(left, shard_rows, preferred_element_type=jnp.float32)  10.1 us
    all_gather x1, waiting for transfers between devices, denoise(): query_all = add_one(lax.all_gather(wq, 'tile', axis=0, tiled=True))  8.64 us
    dot_general x1, matrix products, denoise(): jnp.dot(mixed, lax.all_gather(wo, 'tile', axis=1, tiled=True), preferred_...  6.98 us
  transfers between devices with their start and end apart: 21, of which 19 were waited for; matrix products, arithmetic and copies ran while one was open for 25% of the time, Pallas kernels for 0%

profile of v1, /device:TPU:1, one launch (start us, length us, event | category | flops | bytes accessed | tf_op | source)
XLA Modules:
  0.0 257.5 jit_solution(2343788766092399168)
XLA Ops:
  10.2 1.1 fusion.78
  11.2 2.6 %collective-permute-start = (f32[1,384]{1,0:T(1,128)S(1)}, f32[1,384]{1,0:T(1,128)S(1)}, u32[]{:S(2)}, u32[]{:S(2)}) collective-permute-start(f32[1,384]{1,0:T(1,128)S(1)} %fusion.78), channel_id=1, source_target_pairs={{0,1},{1,2},{2,3},{3,4},{4,5},{5,6},{6,7},{7,8},{8,9},{9,10},{10,1... | collective-permute-start | bytes 4616 | tf_op jit(solution)/shard_map/ppermute | solution.py:23
  14.6 2.3 collective-permute-start.1
  16.9 1.8 collective-permute-done.1
  18.7 1.2 collective-permute-start.2
  19.9 0.8 reduce-window.9
  20.7 3.7 %collective-permute-done.2 = f32[1,384]{1,0:T(1,128)S(1)} collective-permute-done((f32[1,384]{1,0:T(1,128)S(1)}, f32[1,384]{1,0:T(1,128)S(1)}, u32[]{:S(2)}, u32[]{:S(2)}) %collective-permute-start.2) | collective-permute-done | bytes 1568 | tf_op jit(solution)/shard_map/ppermute | solution.py:23
  25.1 5.0 %collective-permute-done.3 = f32[1,384]{1,0:T(1,128)S(1)} collective-permute-done((f32[1,384]{1,0:T(1,128)S(1)}, f32[1,384]{1,0:T(1,128)S(1)}, u32[]{:S(2)}, u32[]{:S(2)}) %collective-permute-start.3) | collective-permute-done | bytes 1568 | tf_op jit(solution)/shard_map/ppermute | solution.py:23
  30.3 5.6 %collective-permute-done.4 = f32[1,384]{1,0:T(1,128)S(1)} collective-permute-done((f32[1,384]{1,0:T(1,128)S(1)}, f32[1,384]{1,0:T(1,128)S(1)}, u32[]{:S(2)}, u32[]{:S(2)}) %collective-permute-start.4) | collective-permute-done | bytes 1568 | tf_op jit(solution)/shard_map/ppermute | solution.py:23
  35.9 5.7 %collective-permute-done.5 = f32[1,384]{1,0:T(1,128)S(1)} collective-permute-done((f32[1,384]{1,0:T(1,128)S(1)}, f32[1,384]{1,0:T(1,128)S(1)}, u32[]{:S(2)}, u32[]{:S(2)}) %collective-permute-start.5) | collective-permute-done | bytes 1568 | tf_op jit(solution)/shard_map/ppermute | solution.py:23
  41.6 5.8 %collective-permute-done.6 = f32[1,384]{1,0:T(1,128)S(1)} collective-permute-done((f32[1,384]{1,0:T(1,128)S(1)}, f32[1,384]{1,0:T(1,128)S(1)}, u32[]{:S(2)}, u32[]{:S(2)}) %collective-permute-start.6) | collective-permute-done | bytes 1568 | tf_op jit(solution)/shard_map/ppermute | solution.py:23
  47.4 1.5 copy.60
  48.9 1.1 copy.61
  50.6 1.5 convert_element_type.57
  53.2 1.1 fusion.75
  54.3 4.6 %collective-permute-done.8 = f32[1,384]{1,0:T(1,128)S(1)} collective-permute-done((f32[1,384]{1,0:T(1,128)S(1)}, f32[1,384]{1,0:T(1,128)S(1)}, u32[]{:S(2)}, u32[]{:S(2)}) %collective-permute-start.8) | collective-permute-done | bytes 1568 | tf_op jit(solution)/shard_map/ppermute | solution.py:23
  58.9 5.7 %collective-permute-done.9 = f32[1,384]{1,0:T(1,128)S(1)} collective-permute-done((f32[1,384]{1,0:T(1,128)S(1)}, f32[1,384]{1,0:T(1,128)S(1)}, u32[]{:S(2)}, u32[]{:S(2)}) %collective-permute-start.9) | collective-permute-done | bytes 1568 | tf_op jit(solution)/shard_map/ppermute | solution.py:23
  64.6 0.8 multiply_reduce_fusion.1
  65.4 4.9 %collective-permute-done.10 = f32[1,384]{1,0:T(1,128)S(1)} collective-permute-done((f32[1,384]{1,0:T(1,128)S(1)}, f32[1,384]{1,0:T(1,128)S(1)}, u32[]{:S(2)}, u32[]{:S(2)}) %collective-permute-start.10) | collective-permute-done | bytes 1568 | tf_op jit(solution)/shard_map/ppermute | solution.py:23
  70.3 5.8 %collective-permute-done.11 = f32[1,384]{1,0:T(1,128)S(1)} collective-permute-done((f32[1,384]{1,0:T(1,128)S(1)}, f32[1,384]{1,0:T(1,128)S(1)}, u32[]{:S(2)}, u32[]{:S(2)}) %collective-permute-start.11) | collective-permute-done | bytes 1568 | tf_op jit(solution)/shard_map/ppermute | solution.py:23
  76.1 5.7 %collective-permute-done.12 = f32[1,384]{1,0:T(1,128)S(1)} collective-permute-done((f32[1,384]{1,0:T(1,128)S(1)}, f32[1,384]{1,0:T(1,128)S(1)}, u32[]{:S(2)}, u32[]{:S(2)}) %collective-permute-start.12) | collective-permute-done | bytes 1568 | tf_op jit(solution)/shard_map/ppermute | solution.py:23
  81.8 5.7 %collective-permute-done.13 = f32[1,384]{1,0:T(1,128)S(1)} collective-permute-done((f32[1,384]{1,0:T(1,128)S(1)}, f32[1,384]{1,0:T(1,128)S(1)}, u32[]{:S(2)}, u32[]{:S(2)}) %collective-permute-start.13) | collective-permute-done | bytes 1568 | tf_op jit(solution)/shard_map/ppermute | solution.py:23
  87.9 5.4 %collective-permute-done.14 = f32[1,384]{1,0:T(1,128)S(1)} collective-permute-done((f32[1,384]{1,0:T(1,128)S(1)}, f32[1,384]{1,0:T(1,128)S(1)}, u32[]{:S(2)}, u32[]{:S(2)}) %collective-permute-start.14) | collective-permute-done | bytes 1568 | tf_op jit(solution)/shard_map/ppermute | solution.py:23
  93.7 5.7 %fusion.4 = bf16[3,256,2048,1]{2,1,3,0:T(8,128)(2,1)} fusion(f32[3,256,2048]{2,1,0:T(8,128)} %copy-done.2, f32[2048]{0:T(1024)S(1)} %bitcast.117, f32[2048]{0:T(1024)S(1)} %bitcast.116, f32[3,256]{1,0:T(4,128)S(1)} %add_rsqrt_fusion.3, f32[3,256]{1,0:T(4,128)S(1)} %broadcast_multiply_fusion.1), kind=kLoop, calls=%fused_computation.13 | loop fusion | flops 7864320 | bytes 9459712 | tf_op jit(solution)/shard_map/convert_element_type | solution.py:112
  99.4 6.5 %copy.64 = bf16[1024,2048]{1,0:T(8,128)(2,1)} copy(bf16[1024,2048]{0,1:T(8,128)(2,1)} %bitcast.107) | data formatting | bytes 8388608 | tf_op jit(solution)/shard_map/dot_general | solution.py:87
  105.9 8.6 %all-gather.7.cloned.1.call-done = bf16[2048,1024]{1,0:T(8,128)(2,1)} async-done(((bf16[128,1024]{1,0:T(8,128)(2,1)}), bf16[2048,1024]{1,0:T(8,128)(2,1)}) %all-gather.7.cloned.1.call-update) | async-done | bytes 4194320 | tf_op jit(solution)/shard_map/all_gather | solution.py:117
  114.6 6.6 %copy.63 = bf16[1024,2048]{1,0:T(8,128)(2,1)} copy(bf16[1024,2048]{0,1:T(8,128)(2,1)} %bitcast.108) | data formatting | bytes 8388608 | tf_op jit(solution)/shard_map/dot_general | solution.py:87
  121.1 44.7 %all-gather.5.cloned.1.call-done = bf16[2048,1024]{1,0:T(8,128)(2,1)} async-done(((bf16[128,1024]{1,0:T(8,128)(2,1)}), bf16[2048,1024]{1,0:T(8,128)(2,1)}) %all-gather.5.cloned.1.call-update) | async-done | bytes 4194320 | tf_op jit(solution)/shard_map/all_gather | solution.py:119
  165.8 6.5 %copy.62 = bf16[1024,2048]{1,0:T(8,128)(2,1)} copy(bf16[1024,2048]{0,1:T(8,128)(2,1)} %bitcast.109) | data formatting | bytes 8388608 | tf_op jit(solution)/shard_map/dot_general | solution.py:87
  172.3 6.6 %multiply_reduce_fusion.3 = (f32[3,256,8]{1,2,0:T(8,128)S(1)}, f32[3,256,8,128]{1,3,2,0:T(8,128)S(1)}) fusion(bf16[3,256,2048,1]{2,1,3,0:T(8,128)(2,1)} %fusion.4, bf16[8,128,2048,1]{2,1,0,3:T(8,128)(2,1)} %bitcast.112), kind=kOutput, calls=%fused_computation.19 | convolution fusion | flops 3222792192 | bytes 10510336 | tf_op jit(solution)/shard_map/dot_general | solution.py:87
  179.0 3.5 %multiply_reduce_fusion.4 = (f32[3,256,8]{1,2,0:T(8,128)S(1)}, f32[3,256,8,128]{1,3,2,0:T(8,128)S(1)}) fusion(bf16[3,256,2048,1]{2,1,3,0:T(8,128)(2,1)S(1)} %copy-done.4, bf16[8,128,2048,1]{2,1,0,3:T(8,128)(2,1)S(1)} %bitcast.111), kind=kOutput, calls=%fused_computation.21 | convolution fusion | flops 3222792192 | bytes 10510336 | tf_op jit(solution)/shard_map/dot_general | solution.py:87
  182.5 1.3 fusion.11
  183.8 4.3 %fusion.76 = (f32[3,8,256]{2,1,0:T(8,128)S(1)}, f32[3,8,256,256]{2,3,1,0:T(8,128)}) fusion(f32[3,8,256,256]{2,3,1,0:T(8,128)S(1)} %fusion.11), kind=kOutput, calls=%fused_computation.165 | output fusion | flops 6291711 | bytes 12607488 | tf_op jit(solution)/shard_map/sub | solution.py:127
  188.1 10.3 %fusion.21 = bf16[3,256,8,128]{1,3,2,0:T(8,128)(2,1)} fusion(f32[3,8,256,256]{2,3,1,0:T(8,128)} %get-tuple-element.26, f32[3,8,256]{2,1,0:T(8,128)S(1)} %get-tuple-element.25, bf16[3,256,2048,1]{2,1,3,0:T(8,128)(2,1)} %fusion.4, bf16[8,128,2048,1]{2,1,0,3:T(8,128)(2,1)} %bitcast.110), kind=kOutput, calls=%fused_computation.38 | convolution fusion | flops 3628597248 | bytes 15228928 | tf_op jit(solution)/shard_map/nhqk,nkhd->nqhd/dot_general | solution.py:129
  198.3 2.0 copy.69
  200.3 19.3 %all-gather.11.cloned.1.call-done = bf16[1024,2048]{1,0:T(8,128)(2,1)} async-done(((bf16[1024,128]{1,0:T(8,128)(2,1)}), bf16[1024,2048]{1,0:T(8,128)(2,1)}) %all-gather.11.cloned.1.call-update) | async-done | bytes 4194320 | tf_op jit(solution)/shard_map/all_gather | solution.py:132
  219.6 7.0 %fusion.77 = (f32[768]{0:T(1024)S(1)}, f32[768,2048]{1,0:T(8,128)S(1)}) fusion(bf16[1024,2048]{1,0:T(8,128)(2,1)} %all-gather.11.cloned.1.call-done, bf16[96,8,8,128]{3,2,1,0:T(8,128)(2,1)S(1)} %bitcast.114, f32[2048]{0:T(1024)S(1)} %bitcast.118, f32[3,256,2048]{2,1,0:T(8,128)} %copy-done.2), kind=kOutput, calls=%fused_computation.166 | convolution fusion | flops 3225943296 | bytes 18361344 | tf_op jit(solution)/shard_map/dot_general | solution.py:131
  226.6 0.8 multiply_reduce_fusion
  227.6 1.1 fusion.25
  229.7 1.1 multiply_bitcast_fusion
  230.8 1.1 copy.70
  232.6 1.6 copy_select_fusion
  234.2 3.2 %collective-permute-start.15 = (f32[32,1,128]{2,0,1:T(8,128)S(1)}, f32[32,1,128]{2,0,1:T(8,128)S(1)}, u32[]{:S(2)}, u32[]{:S(2)}) collective-permute-start(f32[32,1,128]{2,0,1:T(8,128)S(1)} %get-tuple-element.13), channel_id=1, source_target_pairs={{0,1},{1,2},{2,3},{3,4},{4,5},{5,6},{6,7},{7,8},{8,9},{9,10},{10,1... | collective-permute-start | bytes 49160 | tf_op jit(solution)/shard_map/ppermute | solution.py:36
  237.4 2.2 collective-permute-start.16
  239.8 2.6 %collective-permute-done.16 = f32[32,1,128]{2,0,1:T(8,128)S(1)} collective-permute-done((f32[32,1,128]{2,0,1:T(8,128)S(1)}, f32[32,1,128]{2,0,1:T(8,128)S(1)}, u32[]{:S(2)}, u32[]{:S(2)}) %collective-permute-start.16) | collective-permute-done | bytes 16416 | tf_op jit(solution)/shard_map/ppermute | solution.py:39
  247.8 0.9 fusion.42
  248.7 1.1 copy.75
  249.8 1.1 copy.76
  (113 shorter events, 13.4 us)
Async XLA Ops:
  7.2 46.0 %copy-start = (bf16[128,2048]{1,0:T(8,128)(2,1)S(1)}, bf16[128,2048]{1,0:T(8,128)(2,1)}, u32[]{:S(2)}) copy-start(bf16[128,2048]{1,0:T(8,128)(2,1)} %param.22) | copy-start | bytes 1572868
  7.2 92.2 %all-gather.9.cloned.1.call-start = ((), (), s32[]{:S(2)}) async-start(), calls=%async_computation.2 | async-start | bytes 4456448 | tf_op jit(solution)/shard_map/all_gather | solution.py:118
  7.9 106.6 %all-gather.7.cloned.1.call-start = ((), (), s32[]{:S(2)}) async-start(), calls=%async_computation.1 | async-start | bytes 4456448 | tf_op jit(solution)/shard_map/all_gather | solution.py:117
  8.7 157.2 %all-gather.5.cloned.1.call-start = ((), (), s32[]{:S(2)}) async-start(), calls=%async_computation | async-start | bytes 4456448 | tf_op jit(solution)/shard_map/all_gather | solution.py:119
  9.4 210.2 %all-gather.11.cloned.1.call-start = ((), (), s32[]{:S(2)}) async-start(), calls=%async_computation.3 | async-start | bytes 4456448 | tf_op jit(solution)/shard_map/all_gather | solution.py:132
  11.2 3.4 %collective-permute-start = (f32[1,384]{1,0:T(1,128)S(1)}, f32[1,384]{1,0:T(1,128)S(1)}, u32[]{:S(2)}, u32[]{:S(2)}) collective-permute-start(f32[1,384]{1,0:T(1,128)S(1)} %fusion.78), channel_id=1, source_target_pairs={{0,1},{1,2},{2,3},{3,4},{4,5},{5,6},{6,7},{7,8},{8,9},{9,10},{10,1... | collective-permute-start | bytes 4616 | tf_op jit(solution)/shard_map/ppermute | solution.py:23
  14.6 4.0 %collective-permute-start.1 = (f32[1,384]{1,0:T(1,128)S(1)}, f32[1,384]{1,0:T(1,128)S(1)}, u32[]{:S(2)}, u32[]{:S(2)}) collective-permute-start(f32[1,384]{1,0:T(1,128)S(1)} %collective-permute-done), channel_id=1, source_target_pairs={{0,1},{1,2},{2,3},{3,4},{4,5},{5,6},{6,7},{7,8},{8,9},{9,10},{10,1... | collective-permute-start | bytes 4616 | tf_op jit(solution)/shard_map/ppermute | solution.py:23
  18.7 5.8 %collective-permute-start.2 = (f32[1,384]{1,0:T(1,128)S(1)}, f32[1,384]{1,0:T(1,128)S(1)}, u32[]{:S(2)}, u32[]{:S(2)}) collective-permute-start(f32[1,384]{1,0:T(1,128)S(1)} %collective-permute-done.1), channel_id=1, source_target_pairs={{0,1},{1,2},{2,3},{3,4},{4,5},{5,6},{6,7},{7,8},{8,9},{9,10},{10,1... | collective-permute-start | bytes 4616 | tf_op jit(solution)/shard_map/ppermute | solution.py:23
  24.5 5.7 %collective-permute-start.3 = (f32[1,384]{1,0:T(1,128)S(1)}, f32[1,384]{1,0:T(1,128)S(1)}, u32[]{:S(2)}, u32[]{:S(2)}) collective-permute-start(f32[1,384]{1,0:T(1,128)S(1)} %collective-permute-done.2), channel_id=1, source_target_pairs={{0,1},{1,2},{2,3},{3,4},{4,5},{5,6},{6,7},{7,8},{8,9},{9,10},{10,1... | collective-permute-start | bytes 4616 | tf_op jit(solution)/shard_map/ppermute | solution.py:23
  30.2 5.7 %collective-permute-start.4 = (f32[1,384]{1,0:T(1,128)S(1)}, f32[1,384]{1,0:T(1,128)S(1)}, u32[]{:S(2)}, u32[]{:S(2)}) collective-permute-start(f32[1,384]{1,0:T(1,128)S(1)} %collective-permute-done.3), channel_id=1, source_target_pairs={{0,1},{1,2},{2,3},{3,4},{4,5},{5,6},{6,7},{7,8},{8,9},{9,10},{10,1... | collective-permute-start | bytes 4616 | tf_op jit(solution)/shard_map/ppermute | solution.py:23
  35.9 5.7 %collective-permute-start.5 = (f32[1,384]{1,0:T(1,128)S(1)}, f32[1,384]{1,0:T(1,128)S(1)}, u32[]{:S(2)}, u32[]{:S(2)}) collective-permute-start(f32[1,384]{1,0:T(1,128)S(1)} %collective-permute-done.4), channel_id=1, source_target_pairs={{0,1},{1,2},{2,3},{3,4},{4,5},{5,6},{6,7},{7,8},{8,9},{9,10},{10,1... | collective-permute-start | bytes 4616 | tf_op jit(solution)/shard_map/ppermute | solution.py:23
  41.6 5.8 %collective-permute-start.6 = (f32[1,384]{1,0:T(1,128)S(1)}, f32[1,384]{1,0:T(1,128)S(1)}, u32[]{:S(2)}, u32[]{:S(2)}) collective-permute-start(f32[1,384]{1,0:T(1,128)S(1)} %collective-permute-done.5), channel_id=1, source_target_pairs={{0,1},{1,2},{2,3},{3,4},{4,5},{5,6},{6,7},{7,8},{8,9},{9,10},{10,1... | collective-permute-start | bytes 4616 | tf_op jit(solution)/shard_map/ppermute | solution.py:23
  47.4 5.8 %collective-permute-start.7 = (f32[1,384]{1,0:T(1,128)S(1)}, f32[1,384]{1,0:T(1,128)S(1)}, u32[]{:S(2)}, u32[]{:S(2)}) collective-permute-start(f32[1,384]{1,0:T(1,128)S(1)} %collective-permute-done.6), channel_id=1, source_target_pairs={{0,1},{1,2},{2,3},{3,4},{4,5},{5,6},{6,7},{7,8},{8,9},{9,10},{10,1... | collective-permute-start | bytes 4616 | tf_op jit(solution)/shard_map/ppermute | solution.py:23
  53.2 5.7 %collective-permute-start.8 = (f32[1,384]{1,0:T(1,128)S(1)}, f32[1,384]{1,0:T(1,128)S(1)}, u32[]{:S(2)}, u32[]{:S(2)}) collective-permute-start(f32[1,384]{1,0:T(1,128)S(1)} %collective-permute-done.7), channel_id=1, source_target_pairs={{0,1},{1,2},{2,3},{3,4},{4,5},{5,6},{6,7},{7,8},{8,9},{9,10},{10,1... | collective-permute-start | bytes 4616 | tf_op jit(solution)/shard_map/ppermute | solution.py:23
  54.3 11.1 %copy-start.2 = (f32[3,256,2048]{2,1,0:T(8,128)}, f32[3,256,2048]{2,1,0:T(8,128)S(1)}, u32[]{:S(2)}) copy-start(f32[3,256,2048]{2,1,0:T(8,128)S(1)} %get-tuple-element.20) | copy-start | bytes 18874372
  58.9 5.7 %collective-permute-start.9 = (f32[1,384]{1,0:T(1,128)S(1)}, f32[1,384]{1,0:T(1,128)S(1)}, u32[]{:S(2)}, u32[]{:S(2)}) collective-permute-start(f32[1,384]{1,0:T(1,128)S(1)} %collective-permute-done.8), channel_id=1, source_target_pairs={{0,1},{1,2},{2,3},{3,4},{4,5},{5,6},{6,7},{7,8},{8,9},{9,10},{10,1... | collective-permute-start | bytes 4616 | tf_op jit(solution)/shard_map/ppermute | solution.py:23
  64.6 5.7 %collective-permute-start.10 = (f32[1,384]{1,0:T(1,128)S(1)}, f32[1,384]{1,0:T(1,128)S(1)}, u32[]{:S(2)}, u32[]{:S(2)}) collective-permute-start(f32[1,384]{1,0:T(1,128)S(1)} %collective-permute-done.9), channel_id=1, source_target_pairs={{0,1},{1,2},{2,3},{3,4},{4,5},{5,6},{6,7},{7,8},{8,9},{9,10},{10,1... | collective-permute-start | bytes 4616 | tf_op jit(solution)/shard_map/ppermute | solution.py:23
  70.3 5.8 %collective-permute-start.11 = (f32[1,384]{1,0:T(1,128)S(1)}, f32[1,384]{1,0:T(1,128)S(1)}, u32[]{:S(2)}, u32[]{:S(2)}) collective-permute-start(f32[1,384]{1,0:T(1,128)S(1)} %collective-permute-done.10), channel_id=1, source_target_pairs={{0,1},{1,2},{2,3},{3,4},{4,5},{5,6},{6,7},{7,8},{8,9},{9,10},{10,1... | collective-permute-start | bytes 4616 | tf_op jit(solution)/shard_map/ppermute | solution.py:23
  76.1 5.7 %collective-permute-start.12 = (f32[1,384]{1,0:T(1,128)S(1)}, f32[1,384]{1,0:T(1,128)S(1)}, u32[]{:S(2)}, u32[]{:S(2)}) collective-permute-start(f32[1,384]{1,0:T(1,128)S(1)} %collective-permute-done.11), channel_id=1, source_target_pairs={{0,1},{1,2},{2,3},{3,4},{4,5},{5,6},{6,7},{7,8},{8,9},{9,10},{10,1... | collective-permute-start | bytes 4616 | tf_op jit(solution)/shard_map/ppermute | solution.py:23
  81.8 5.7 %collective-permute-start.13 = (f32[1,384]{1,0:T(1,128)S(1)}, f32[1,384]{1,0:T(1,128)S(1)}, u32[]{:S(2)}, u32[]{:S(2)}) collective-permute-start(f32[1,384]{1,0:T(1,128)S(1)} %collective-permute-done.12), channel_id=1, source_target_pairs={{0,1},{1,2},{2,3},{3,4},{4,5},{5,6},{6,7},{7,8},{8,9},{9,10},{10,1... | collective-permute-start | bytes 4616 | tf_op jit(solution)/shard_map/ppermute | solution.py:23
  87.5 5.7 %collective-permute-start.14 = (f32[1,384]{1,0:T(1,128)S(1)}, f32[1,384]{1,0:T(1,128)S(1)}, u32[]{:S(2)}, u32[]{:S(2)}) collective-permute-start(f32[1,384]{1,0:T(1,128)S(1)} %collective-permute-done.13), channel_id=1, source_target_pairs={{0,1},{1,2},{2,3},{3,4},{4,5},{5,6},{6,7},{7,8},{8,9},{9,10},{10,1... | collective-permute-start | bytes 4616 | tf_op jit(solution)/shard_map/ppermute | solution.py:23
  172.3 6.7 %copy-start.3 = (bf16[1024,2048]{1,0:T(8,128)(2,1)S(1)}, bf16[1024,2048]{1,0:T(8,128)(2,1)}, u32[]{:S(2)}) copy-start(bf16[1024,2048]{1,0:T(8,128)(2,1)} %copy.63) | copy-start | bytes 12582916
  172.3 6.7 %copy-start.4 = (bf16[3,256,2048,1]{2,1,3,0:T(8,128)(2,1)S(1)}, bf16[3,256,2048,1]{2,1,3,0:T(8,128)(2,1)}, u32[]{:S(2)}) copy-start(bf16[3,256,2048,1]{2,1,3,0:T(8,128)(2,1)} %fusion.4) | copy-start | bytes 9437188
  178.9 3.5 %copy-start.9 = (f32[128]{0:T(128)S(1)}, f32[128]{0:T(128)}, u32[]{:S(2)}) copy-start(f32[128]{0:T(128)} %param.29) | copy-start | bytes 1540
  179.0 3.5 %copy-start.10 = (f32[128]{0:T(128)S(1)}, f32[128]{0:T(128)}, u32[]{:S(2)}) copy-start(f32[128]{0:T(128)} %param.28) | copy-start | bytes 1540
  226.6 1.0 copy-start.7
  230.8 1.8 copy-start.5
  232.0 10.8 %copy-start.8 = (f32[9,32,32]{2,1,0:T(8,128)S(1)}, f32[9,32,32]{2,1,0:T(8,128)}, u32[]{:S(2)}) copy-start(f32[9,32,32]{2,1,0:T(8,128)} %param.31) | copy-start | bytes 110596
  234.2 5.6 %collective-permute-start.15 = (f32[32,1,128]{2,0,1:T(8,128)S(1)}, f32[32,1,128]{2,0,1:T(8,128)S(1)}, u32[]{:S(2)}, u32[]{:S(2)}) collective-permute-start(f32[32,1,128]{2,0,1:T(8,128)S(1)} %get-tuple-element.13), channel_id=1, source_target_pairs={{0,1},{1,2},{2,3},{3,4},{4,5},{5,6},{6,7},{7,8},{8,9},{9,10},{10,1... | collective-permute-start | bytes 49160 | tf_op jit(solution)/shard_map/ppermute | solution.py:36
  237.4 5.1 %collective-permute-start.16 = (f32[32,1,128]{2,0,1:T(8,128)S(1)}, f32[32,1,128]{2,0,1:T(8,128)S(1)}, u32[]{:S(2)}, u32[]{:S(2)}) collective-permute-start(f32[32,1,128]{2,0,1:T(8,128)S(1)} %get-tuple-element.14), channel_id=1, source_target_pairs={{1,0},{2,1},{3,2},{4,3},{5,4},{6,5},{7,6},{8,7},{9,8},{10,9},{11,1... | collective-permute-start | bytes 49160 | tf_op jit(solution)/shard_map/ppermute | solution.py:39
  245.4 2.5 copy-start.6
  247.2 3.7 %copy-start.1 = (bf16[128,2048]{1,0:T(8,128)(2,1)S(1)}, bf16[128,2048]{1,0:T(8,128)(2,1)}, u32[]{:S(2)}) copy-start(bf16[128,2048]{1,0:T(8,128)(2,1)} %param.22) | copy-start | bytes 1572868
Sparse Core Ops, SparseCore 0:
  10.2 53.0 all-gather.8
  65.5 49.0 all-gather.6
  116.7 49.0 all-gather.4
  167.8 51.7 all-gather.10
